TPU v7x, 256 devices: a whole 4x4x8 slice. The times are simulated.
256 devices in a mesh: seq: 16 (over z, core), head: 16 (over x, y).
Axes of the slice: x: 4, y: 4, z: 8, core: 2. Of those that a mesh axis runs over, the one named last changes fastest.
Arguments:
- hidden_in: bfloat16 [4, 128, 2048], P(None, None, 'seq'), may hold values from -6 to 6
- attn_gain: float32 [2048], P('seq'), may hold values from 0.1 to 1.9
- attn_router: bfloat16 [2048, 8], P('seq'), may hold values from -0.125 to 0.125
- query_weight: bfloat16 [2048, 8, 2048], P('seq', None, 'head'), may hold values from -0.125 to 0.125
- kv_weight: bfloat16 [2048, 4096], P('seq', 'head'), may hold values from -0.125 to 0.125
- out_weight: bfloat16 [8, 2048, 2048], P(None, 'head', 'seq'), may hold values from -0.09375 to 0.09375
- mlp_gain: float32 [2048], replicated, may hold values from 0.1 to 1.9
- mlp_router: bfloat16 [2048, 8], replicated, may hold values from -0.125 to 0.125
- gate_weight: bfloat16 [2048, 45056], P(None, ('seq', 'head')), may hold values from -0.125 to 0.125
- up_weight: bfloat16 [2048, 45056], P(None, ('seq', 'head')), may hold values from -0.125 to 0.125
- down_weight: bfloat16 [45056, 2048], P(('seq', 'head')), may hold values from -0.3125 to 0.3125
- cache: bfloat16 [196608, 4096], P('seq', 'head'), as said below
- token_req: int32 [196608], P('seq'), may hold values from -1 to 127, as said below
- attn_route: int32 [4, 128, 2], replicated, may hold values from 0 to 7, all different within a row
- mlp_route: int32 [4, 128, 2], replicated, may hold values from 0 to 7, all different within a row; in each aligned block of 512 rows (0 to 511, 512 to 1023, ..., all dimensions but the last counted through in order) at most 192 rows name the same one
- owner: int32 [128], replicated, may hold values from 0 to 15, as said below
Outputs:
- hidden_out: bfloat16 [4, 128, 2048], P(None, 'head', 'seq')
- new_cache: bfloat16 [160, 4, 4096], P('seq', None, 'head')
Inputs may be any that keep to these rules, and one draw needn't show every extreme that they name: `token_req`: slots form pages of 128; the live slots of a page belong to one request; request r has lengths[r] live slots; four requests have exactly 32768, every other at least one and less than 512. At most 10 requests share an owner, and some owner has exactly 10. `cache`: rows of empty slots hold values too. `attn_route`: the 2 experts of a token differ. `mlp_route`: the 2 experts of a token differ; over all 4 x 128 tokens no expert is chosen more than 192 times, and one is chosen exactly 192 times.
All inputs are finite; a program needn't handle non-finite values.
Results may differ from a plain program's by a relative error of at most 0.019.
Values may be sent and summed in bfloat16 or wider, within the bound.
No kernel may reach another device: no remote copies, remote signals or barrier semaphores. Data moves between devices by JAX's collectives and lax.ppermute only.
A program may use at most 64 MiB of HBM per device.

v0:
```python
import math
import jax
import jax.numpy as jnp
from jax import lax
from jax.sharding import PartitionSpec as P

D = 2048
HD = 128
FF = 5632
PAGE = 128
OWN_MAX = 10
epsilon = 1e-06
masked_score = -1e30


def frequency(width):
    return jnp.power(jnp.float32(10000.0), -2.0 * jnp.arange(width // 2, dtype=jnp.float32) / width)


def rotate(values, angles):
    half_width = values.shape[-1] // 2
    cosine = jnp.cos(angles)
    sine_part = jnp.sin(angles)
    lower_half = values[..., :half_width]
    upper_half = values[..., half_width:]
    return jnp.concatenate(
        [
            lower_half * cosine - upper_half * sine_part,
            upper_half * cosine + lower_half * sine_part,
        ],
        axis=-1,
    )


def on_device(
    hidden_in,
    attn_gain,
    attn_router,
    query_weight,
    kv_weight,
    out_weight,
    mlp_gain,
    mlp_router,
    gate_weight,
    up_weight,
    down_weight,
    cache,
    token_req,
    attn_route,
    mlp_route,
    owner,
):
    highest = lax.Precision.HIGHEST
    step_count, req_count, local_width = hidden_in.shape
    head_count = lax.axis_size("head")
    seq_index = lax.axis_index("seq")
    head_index = lax.axis_index("head")
    experts = query_weight.shape[1]
    heads_dev = kv_weight.shape[1] // (2 * HD)
    top_count = attn_route.shape[2]
    tok_rows = step_count * req_count
    queries_all = step_count * top_count
    hidden_f = hidden_in.astype(jnp.float32)
    squares = jnp.sum(hidden_f * hidden_f, axis=2)
    scaled = (hidden_f * attn_gain).astype(jnp.bfloat16).reshape(tok_rows, local_width)
    query_part = jnp.dot(
        scaled,
        query_weight.reshape(local_width, experts * heads_dev * HD),
        preferred_element_type=jnp.float32,
    ).reshape(step_count, req_count, experts, heads_dev * HD)
    kv_part = jnp.dot(scaled, kv_weight, preferred_element_type=jnp.float32).reshape(
        step_count, req_count, heads_dev * 2 * HD
    )
    logit_part = jnp.dot(scaled, attn_router, preferred_element_type=jnp.float32).reshape(
        step_count, req_count, experts
    )
    request_ids = jnp.arange(req_count, dtype=jnp.int32)
    counts = jnp.sum((token_req[:, None] == request_ids[None, :]).astype(jnp.float32), axis=0)
    attn_hot = (attn_route[..., None] == jnp.arange(experts, dtype=jnp.int32)).astype(jnp.float32)
    query_sum, kv_sum, logit_sum, square_sum, lengths = lax.psum(
        (query_part, kv_part, logit_part, squares, counts), "seq"
    )
    picked = jnp.einsum("srke,srec->srkc", attn_hot, query_sum, precision=highest)
    inverse = lax.rsqrt(square_sum / D + epsilon)
    attn_gates = jax.nn.softmax(
        jnp.sum(attn_hot * (logit_sum * inverse[..., None])[:, :, None, :], axis=3), axis=2
    )
    positions = lengths[None, :] + jnp.arange(step_count, dtype=jnp.float32)[:, None]
    freq_table = frequency(HD)
    queries = (picked * inverse[..., None, None]).reshape(
        step_count, req_count, top_count, heads_dev, HD
    )
    queries = rotate(queries, positions[:, :, None, None, None] * freq_table).astype(jnp.bfloat16)
    projected = kv_sum.reshape(step_count, req_count, heads_dev, 2 * HD) * inverse[..., None, None]
    new_keys = rotate(projected[..., :HD], positions[:, :, None, None] * freq_table).astype(
        jnp.bfloat16
    )
    new_values = projected[..., HD:].astype(jnp.bfloat16)
    new_rows = jnp.concatenate([new_keys, new_values], axis=3).reshape(
        step_count, req_count, heads_dev * 2 * HD
    )
    owned_flag = (owner == seq_index).astype(jnp.int32)
    before = (request_ids[None, :] < request_ids[:, None]).astype(jnp.int32)
    slot_rank = jnp.sum(before * owned_flag[None, :], axis=1)
    slot_ids = jnp.arange(OWN_MAX, dtype=jnp.int32)
    select = ((owned_flag[None, :] == 1) & (slot_rank[None, :] == slot_ids[:, None])).astype(
        jnp.bfloat16
    )
    appended = jnp.einsum(
        "jr,src->jsc", select, new_rows, preferred_element_type=jnp.float32
    ).astype(jnp.bfloat16)
    page_total = token_req.shape[0] // PAGE
    page_owner = token_req.reshape(page_total, PAGE)
    page_req = jnp.max(page_owner, axis=1)
    page_pick = jnp.maximum(page_req, 0)
    live_slot = page_owner >= 0
    req_hot = (page_req[None, :] == request_ids[:, None]).astype(jnp.float32)
    query_rows = jnp.transpose(queries, (1, 3, 0, 2, 4)).reshape(
        req_count, heads_dev, queries_all, HD
    )
    page_queries = query_rows[page_pick]
    paged = cache.reshape(page_total, PAGE, heads_dev, 2 * HD)
    score_scale = 1.0 / math.sqrt(HD)
    scores = (
        jnp.einsum(
            "phqd,pthd->phqt", page_queries, paged[..., :HD], preferred_element_type=jnp.float32
        )
        * score_scale
    )
    scores = jnp.where(live_slot[:, None, None, :], scores, masked_score)
    fresh_keys = jnp.transpose(new_keys, (1, 2, 0, 3))
    fresh_values = jnp.transpose(new_values, (1, 2, 0, 3))
    fresh_scores = (
        jnp.einsum("rhqd,rhsd->rhqs", query_rows, fresh_keys, preferred_element_type=jnp.float32)
        * score_scale
    )
    query_step = jnp.arange(queries_all) // top_count
    causal = jnp.arange(step_count)[None, :] <= query_step[:, None]
    fresh_live = causal[None, None, :, :] & (owned_flag[:, None, None, None] == 1)
    fresh_scores = jnp.where(fresh_live, fresh_scores, masked_score)
    page_best = jnp.max(scores, axis=3)
    local_best = jnp.max(
        jnp.where(req_hot[:, :, None, None] > 0, page_best[None], masked_score), axis=1
    )
    local_best = jnp.maximum(local_best, jnp.max(fresh_scores, axis=3))
    maxima = lax.pmax(local_best, "seq")
    page_probs = jnp.where(
        live_slot[:, None, None, :], jnp.exp(scores - maxima[page_pick][..., None]), 0.0
    )
    page_sums = jnp.sum(page_probs, axis=3)
    page_out = jnp.einsum(
        "phqt,pthd->phqd",
        page_probs.astype(jnp.bfloat16),
        paged[..., HD:],
        preferred_element_type=jnp.float32,
    )
    fresh_probs = jnp.where(fresh_live, jnp.exp(fresh_scores - maxima[..., None]), 0.0)
    totals = jnp.einsum("rp,phq->rhq", req_hot, page_sums, precision=highest) + jnp.sum(
        fresh_probs, axis=3
    )
    outputs = jnp.einsum("rp,phqd->rhqd", req_hot, page_out, precision=highest)
    outputs = outputs + jnp.einsum(
        "rhqs,rhsd->rhqd",
        fresh_probs.astype(jnp.bfloat16),
        fresh_values,
        preferred_element_type=jnp.float32,
    )
    local_totals = totals
    local_outputs = outputs
    totals, outputs = (
        lax.psum(local_totals.astype(jnp.bfloat16), "seq").astype(jnp.float32),
        lax.psum(local_outputs.astype(jnp.bfloat16), "seq").astype(jnp.float32),
    )
    attention = outputs / totals[..., None]
    attention = jnp.transpose(
        attention.reshape(req_count, heads_dev, step_count, top_count, HD), (2, 0, 3, 1, 4)
    )
    weighted = (attention * attn_gates[..., None, None]).astype(jnp.bfloat16)
    mixed = jnp.einsum(
        "srkhd,srke->srehd", weighted.astype(jnp.float32), attn_hot, precision=highest
    ).astype(jnp.bfloat16)
    head_part = jnp.dot(
        mixed.reshape(tok_rows, experts * heads_dev * HD),
        out_weight.reshape(experts * heads_dev * HD, local_width),
        preferred_element_type=jnp.float32,
    ).reshape(step_count, req_count, local_width)
    attn_out = lax.psum(head_part.astype(jnp.bfloat16), "head").astype(jnp.float32)
    residual = (hidden_f + attn_out).astype(jnp.bfloat16)
    full_rows = lax.all_gather(residual, "seq", axis=2, tiled=True)
    full_f = full_rows.astype(jnp.float32)
    inverse_mlp = lax.rsqrt(jnp.mean(full_f * full_f, axis=2) + epsilon)
    normed = (full_f * inverse_mlp[..., None] * mlp_gain).astype(jnp.bfloat16).reshape(tok_rows, D)
    mlp_logits = jnp.dot(normed, mlp_router, preferred_element_type=jnp.float32).reshape(
        step_count, req_count, experts
    )
    mlp_hot = (mlp_route[..., None] == jnp.arange(experts, dtype=jnp.int32)).astype(jnp.float32)
    mlp_gates = jax.nn.softmax(jnp.sum(mlp_hot * mlp_logits[:, :, None, :], axis=3), axis=2)
    combine_w = jnp.sum(mlp_hot * mlp_gates[..., None], axis=2)
    unit_count = gate_weight.shape[1]
    device_index = seq_index * head_count + head_index
    expert_index = device_index * unit_count // FF
    expert_ids = jnp.arange(experts, dtype=jnp.int32)
    rows_dev = req_count // head_count
    expert_weight = jnp.sum(
        combine_w * (expert_ids == expert_index).astype(jnp.float32), axis=2
    ).reshape(tok_rows, 1)
    gate_pre = jnp.dot(normed, gate_weight, preferred_element_type=jnp.float32)
    up_pre = jnp.dot(normed, up_weight, preferred_element_type=jnp.float32)
    hidden_units = (jax.nn.silu(gate_pre) * up_pre).astype(jnp.bfloat16)
    expert_term = (
        jnp.dot(hidden_units, down_weight, preferred_element_type=jnp.float32) * expert_weight
    ).reshape(step_count, req_count, D)
    by_columns = lax.psum_scatter(
        expert_term.astype(jnp.bfloat16), "seq", scatter_dimension=2, tiled=True
    )
    expert_part = lax.psum_scatter(by_columns, "head", scatter_dimension=1, tiled=True).astype(
        jnp.float32
    )
    own_rows = lax.dynamic_slice_in_dim(residual, head_index * rows_dev, rows_dev, 1)
    hidden_out = (own_rows.astype(jnp.float32) + expert_part).astype(jnp.bfloat16)
    return (hidden_out, appended)


def solution(mesh):
    in_specs = (
        P(None, None, "seq"),
        P("seq"),
        P("seq", None),
        P("seq", None, "head"),
        P("seq", "head"),
        P(None, "head", "seq"),
        P(),
        P(),
        P(None, ("seq", "head")),
        P(None, ("seq", "head")),
        P(("seq", "head"), None),
        P("seq", "head"),
        P("seq"),
        P(),
        P(),
        P(),
    )
    out_specs = (P(None, "head", "seq"), P("seq", None, "head"))
    return jax.shard_map(
        on_device, mesh=mesh, in_specs=in_specs, out_specs=out_specs, check_vma=False
    )
```

profile of v0, /device:TPU:2, one launch (start us, length us, event | category | flops | bytes accessed | tf_op | source)
XLA Modules:
  0.0 634.6 jit_solution(8452154288114500692)
XLA Ops:
  7.2 1.1 copy.167
  8.3 0.2 copy.112
  8.5 2.0 fusion.79
  10.4 2.7 fusion.67
  13.2 0.1 fusion.46
  13.4 5.5 convert_reduce_fusion
  18.9 0.1 bitcast_reduce_fusion
  19.1 0.1 fusion.77
  19.2 50.9 %all-reduce.1 = (f32[4,128]{1,0:T(4,128)S(1)}, f32[128]{0:T(128)S(1)}, f32[4,128,8]{1,2,0:T(8,128)S(1)}) all-reduce(f32[4,128]{1,0:T(4,128)S(1)} %fusion.46, f32[128]{0:T(128)S(1)} %convert_reduce_fusion, f32[4,128,8]{1,2,0:T(8,128)S(1)} %fusion.77), channel_id=1, replica_groups=mesh['seq'=16,'head'=16] {'seq'}, use_global_device_ids=true, to_apply=%region_3.0 | all-reduce | flops 4736 | bytes 37888 | tf_op jit(solution)/shard_map/psum | solution.py:80
  70.2 0.1 copy.111
  70.4 0.1 copy.124
  70.6 7.3 %select_reduce_fusion.2 = f32[4,128,2]{2,1,0:T(8,128)S(1)} fusion(f32[4,128,8]{2,1,0:T(8,128)S(1)} %copy.124, s32[4,128,2]{2,1,0:T(8,128)S(1)} %copy.111), kind=kLoop, calls=%fused_computation.46 | loop fusion | flops 23552 | bytes 24576 | tf_op jit(solution)/shard_map/reduce_sum | solution.py:86
  77.8 0.8 fusion.103
  78.6 0.1 broadcast_divide_fusion
  78.8 1.0 multiply_cosine_fusion.1
  79.8 53.4 %all-reduce.14.cloned.1.call-done = (f32[4,128,256]{2,1,0:T(8,128)}, f32[4,128,8,128]{3,1,2,0:T(8,128)}) async-done(((f32[4,128,256]{2,1,0:T(8,128)}, f32[4,128,8,128]{3,1,2,0:T(8,128)}), (f32[4,128,256]{2,1,0:T(8,128)}, f32[4,128,8,128]{3,1,2,0:T(8,128)})) %all-reduce.14.cloned.1.call-update) | async-done | bytes 2621456 | tf_op jit(solution)/shard_map/psum | solution.py:80
  133.2 1.3 multiply_bitcast_fusion
  134.5 1.2 fusion.42
  135.8 3.2 fusion.12
  138.9 0.8 subtract_convert_fusion
  139.8 0.7 maximum_bitcast_fusion
  140.6 0.2 copy.115
  140.7 0.7 gather_fusion
  141.4 3.7 fusion.101
  145.1 0.2 select_reduce_fusion.3
  145.4 0.1 maximum_bitcast_fusion.3
  145.5 0.5 fusion.102
  146.0 48.3 %pmax.7 = f32[128,1,8]{2,0,1:T(8,128)S(1)} all-reduce(f32[128,1,8]{2,0,1:T(8,128)S(1)} %maximum_bitcast_fusion.4), channel_id=1, replica_groups=mesh['seq'=16,'head'=16] {'seq'}, use_global_device_ids=true, to_apply=%region_10.0 | all-reduce | flops 1024 | bytes 8192 | tf_op jit(solution)/shard_map/pmax | solution.py:146
  194.3 0.6 gather_fusion.1
  194.9 2.9 fusion.5
  197.7 0.3 fusion.39
  198.1 0.3 fusion.63
  198.4 0.7 fusion.65
  199.1 1.3 fusion.21
  200.5 0.2 fusion.26
  200.7 23.6 %psum.61 = bf16[128,8]{0,1:T(8,128)(2,1)S(1)} all-reduce(bf16[128,8]{0,1:T(8,128)(2,1)S(1)} %fusion.26), channel_id=1, replica_groups=mesh['seq'=16,'head'=16] {'seq'}, use_global_device_ids=true, to_apply=%region_14.15 | all-reduce | flops 1024 | bytes 4096 | tf_op jit(solution)/shard_map/psum | solution.py:171
  224.3 83.3 %all-reduce.8.cloned.1.call-done = bf16[128,1,8,128]{3,0,2,1:T(8,128)(2,1)} async-done(((bf16[128,1,8,128]{3,0,2,1:T(8,128)(2,1)}), bf16[128,1,8,128]{3,0,2,1:T(8,128)(2,1)}) %all-reduce.8.cloned.1.call-update) | async-done | bytes 262160 | tf_op jit(solution)/shard_map/psum | solution.py:172
  307.6 1.2 convert_divide_fusion
  308.8 2.7 convolution_convert_fusion
  311.6 1.1 fusion.25
  312.7 92.5 %all-reduce.10.cloned.1.call-done = bf16[4,128,128]{2,1,0:T(8,128)(2,1)} async-done(((bf16[4,128,128]{2,1,0:T(8,128)(2,1)}), bf16[4,128,128]{2,1,0:T(8,128)(2,1)}) %all-reduce.10.cloned.1.call-update) | async-done | bytes 131088 | tf_op jit(solution)/shard_map/psum | solution.py:187
  405.2 1.6 fusion.47
  406.9 0.1 copy.126
  407.1 40.6 %all-gather.2.cloned.1.call-done = bf16[4,128,2048]{2,1,0:T(8,128)(2,1)} async-done(((bf16[4,128,128]{2,1,0:T(8,128)(2,1)}), bf16[4,128,2048]{2,1,0:T(8,128)(2,1)}) %all-gather.2.cloned.1.call-update) | async-done | bytes 2097168 | tf_op jit(solution)/shard_map/all_gather | solution.py:189
  447.7 2.2 fusion.2
  450.0 0.5 fusion.4
  450.5 1.3 copy-done.2
  451.9 0.7 fusion.85
  452.6 7.3 %select_reduce_fusion.1 = f32[4,128,2]{2,1,0:T(8,128)S(1)} fusion(f32[4,128,8]{2,1,0:T(8,128)S(1)} %fusion.85, s32[4,128,2]{2,1,0:T(8,128)S(1)} %copy.126), kind=kLoop, calls=%fused_computation.44 | loop fusion | flops 23552 | bytes 24576 | tf_op jit(solution)/shard_map/reduce_sum | solution.py:197
  459.8 0.2 fusion.72
  460.1 1.4 select_reduce_fusion
  461.7 3.5 fusion.104
  465.2 4.1 multiply_convert_fusion
  469.4 3.1 copy.133
  472.5 1.7 copy.166
  474.3 0.6 copy-done.17
  474.9 0.6 dynamic-slice
  476.2 56.6 %reduce-scatter.5.cloned.1.call-done = bf16[128,512]{1,0:T(8,128)(2,1)} async-done(((bf16[2048,512]{1,0:T(8,128)(2,1)}), bf16[128,512]{1,0:T(8,128)(2,1)}) %reduce-scatter.5.cloned.1.call-update) | async-done | bytes 131088
  532.9 0.9 reshape.447
  533.8 0.8 copy.134
  534.6 0.3 convolution_convert_fusion.1
  534.9 0.6 copy.129
  535.5 91.0 %all-reduce.12.cloned.1.call-done = bf16[4,128,128]{2,1,0:T(8,128)(2,1)} async-done(((bf16[4,128,128]{2,1,0:T(8,128)(2,1)}), bf16[4,128,128]{2,1,0:T(8,128)(2,1)}) %all-reduce.12.cloned.1.call-update) | async-done | bytes 131088
  626.5 1.3 add_convert_fusion.1
  (68 shorter events, 1.1 us)
Async XLA Ops:
  7.2 458.1 %copy-start = (bf16[176,2048]{1,0:T(8,128)(2,1)S(1)}, bf16[176,2048]{1,0:T(8,128)(2,1)}, u32[]{:S(2)}) copy-start(bf16[176,2048]{1,0:T(8,128)(2,1)} %param.26) | copy-start | bytes 2162692
  7.2 126.0 %all-reduce.14.cloned.1.call-start = ((), (), s32[]{:S(2)}) async-start(), calls=%async_computation.6 | async-start | bytes 5242880 | tf_op jit(solution)/shard_map/psum | solution.py:80
  10.4 2.8 copy-start.4
  10.4 3.0 copy-start.7
  10.4 8.7 %copy-start.11 = (f32[128]{0:T(128)S(1)}, f32[128]{0:T(128)}, u32[]{:S(2)}) copy-start(f32[128]{0:T(128)} %param.17) | copy-start | bytes 1540
  10.4 8.7 %copy-start.16 = (bf16[128,8]{0,1:T(8,128)(2,1)S(1)}, bf16[128,8]{0,1:T(8,128)(2,1)}, u32[]{:S(2)}) copy-start(bf16[128,8]{0,1:T(8,128)(2,1)} %param.18) | copy-start | bytes 6148
  13.1 57.1 %copy-start.12 = (s32[128]{0:T(128)S(1)}, s32[128]{0:T(128)}, u32[]{:S(2)}) copy-start(s32[128]{0:T(128)} %param.31) | copy-start | bytes 1540
  13.1 57.1 %copy-start.9 = (s32[4,128,2]{1,2,0:T(2,128)S(1)}, s32[4,128,2]{1,2,0:T(2,128)}, u32[]{:S(2)}) copy-start(s32[4,128,2]{1,2,0:T(2,128)} %param.29) | copy-start | bytes 12292
  13.2 294.5 %all-reduce.8.cloned.1.call-start = ((), (), s32[]{:S(2)}) async-start(), calls=%async_computation.1 | async-start | bytes 524288 | tf_op jit(solution)/shard_map/psum | solution.py:172
  133.2 2.6 copy-start.13
  135.7 9.7 %copy-start.5 = (bf16[4,128,1,64]{3,1,0,2:T(8,128)(2,1)}, bf16[4,128,1,64]{3,1,0,2:T(8,128)(2,1)S(1)}, u32[]{:S(2)}) copy-start(bf16[4,128,1,64]{3,1,0,2:T(8,128)(2,1)S(1)} %get-tuple-element.26) | copy-start | bytes 196612
  200.4 204.9 %all-reduce.10.cloned.1.call-start = ((), (), s32[]{:S(2)}) async-start(), calls=%async_computation.2 | async-start | bytes 262144 | tf_op jit(solution)/shard_map/psum | solution.py:187
  308.8 2.7 copy-start.14
  311.5 95.4 %copy-start.10 = (s32[4,128,2]{1,2,0:T(2,128)S(1)}, s32[4,128,2]{1,2,0:T(2,128)}, u32[]{:S(2)}) copy-start(s32[4,128,2]{1,2,0:T(2,128)} %param.30) | copy-start | bytes 12292
  311.6 138.4 %copy-start.8 = (f32[2048]{0:T(1024)S(1)}, f32[2048]{0:T(1024)}, u32[]{:S(2)}) copy-start(f32[2048]{0:T(1024)} %param.22) | copy-start | bytes 24580
  312.7 135.0 %all-gather.2.cloned.1.call-start = ((), (), s32[]{:S(2)}) async-start(), calls=%async_computation.3 | async-start | bytes 2228224 | tf_op jit(solution)/shard_map/all_gather | solution.py:189
  406.8 126.0 %reduce-scatter.5.cloned.1.call-start = ((), (), s32[]{:S(2)}) async-start(), calls=%async_computation.4 | async-start | bytes 2228224
  447.7 2.2 copy-start.1
  450.0 1.9 copy-start.15
  450.5 1.4 copy-start.2
  461.7 3.5 copy-start.3
  474.2 0.7 copy-start.17
  474.2 60.4 %copy-start.6 = (bf16[4,128,1,64]{3,1,0,2:T(8,128)(2,1)S(1)}, bf16[4,128,1,64]{3,1,0,2:T(8,128)(2,1)}, u32[]{:S(2)}) copy-start(bf16[4,128,1,64]{3,1,0,2:T(8,128)(2,1)} %copy-done.5) | copy-start | bytes 196612
  474.2 152.2 %all-reduce.12.cloned.1.call-start = ((), (), s32[]{:S(2)}) async-start(), calls=%async_computation.5 | async-start | bytes 262144
Sparse Core Ops, SparseCore 0:
  13.3 119.8 all-reduce.13
  200.5 107.0 all-reduce.7
  312.8 92.3 all-reduce.9
  407.0 40.6 all-gather.1
  474.3 58.4 reduce-scatter.4
  535.9 90.5 all-reduce.11
where the time goes:
time: 635 us
  waiting for transfers between devices  418 us (66%)
  blocking collectives  123 us (19%)
  other arithmetic  36 us (6%)
  matrix products  29.6 us (5%)
  between operations  15.3 us (2%)
  local copies, waits for them, and re-layouts  13.2 us (2%)
    unnamed x8, waiting for transfers between devices  148 us
    psum x1, waiting for transfers between devices, on_device(): lax.psum(head_part.astype(jnp.bfloat16), 'head').astype(jnp.float32)  92.5 us
    psum x1, waiting for transfers between devices, on_device(): lax.psum(local_outputs.astype(jnp.bfloat16), 'seq').astype(jnp.float32)  83.3 us
    psum x1, waiting for transfers between devices, on_device(): lax.psum((query_part, kv_part, logit_part, squares, counts), 'seq')  53.4 us
    psum x1, blocking collectives, on_device(): lax.psum((query_part, kv_part, logit_part, squares, counts), 'seq')  50.9 us
    pmax x1, blocking collectives, on_device(): maxima = lax.pmax(local_best, 'seq')  48.3 us
    all_gather x1, waiting for transfers between devices, on_device(): full_rows = lax.all_gather(residual, 'seq', axis=2, tiled=True)  40.6 us
    psum x1, blocking collectives, on_device(): lax.psum(local_totals.astype(jnp.bfloat16), 'seq').astype(jnp.float32)  23.6 us
  transfers between devices with their start and end apart: 6, of which 6 were waited for; matrix products, arithmetic and copies ran while one was open for 3% of the time, Pallas kernels for 0%

commit v1 on v0

--- a/solution.py
+++ b/solution.py
@@ -186,7 +186,9 @@
     ).reshape(step_count, req_count, local_width)
     attn_out = lax.psum(head_part.astype(jnp.bfloat16), "head").astype(jnp.float32)
     residual = (hidden_f + attn_out).astype(jnp.bfloat16)
-    full_rows = lax.all_gather(residual, "seq", axis=2, tiled=True)
+    full_rows = jnp.concatenate(
+        lax.all_to_all(jnp.stack([residual] * lax.axis_size("seq")), "seq", 0, 0), axis=2
+    )
     full_f = full_rows.astype(jnp.float32)
     inverse_mlp = lax.rsqrt(jnp.mean(full_f * full_f, axis=2) + epsilon)
     normed = (full_f * inverse_mlp[..., None] * mlp_gain).astype(jnp.bfloat16).reshape(tok_rows, D)

time: 635 us -> 661 us (1.041)
  local copies, waits for them, and re-layouts: 13.2 us -> 23.2 us
  starting transfers between devices: 0.25 us -> 7.5 us
    all_to_all x0 -> x1, waiting for transfers between devices: none -> 48.3 us  [on_device(): lax.all_to_all(jnp.stack([residual] * lax.axis_size('seq')), 'seq', 0, 0)]
    all_gather x1 -> x0, waiting for transfers between devices: 40.6 us -> none  [on_device(): full_rows = lax.all_gather(residual, 'seq', axis=2, tiled=True)]
    all_to_all x0 -> x1, starting transfers between devices: none -> 7.3 us  [on_device(): lax.all_to_all(jnp.stack([residual] * lax.axis_size('seq')), 'seq', 0, 0)]
    unnamed x8 -> x7, waiting for transfers between devices: 148 us -> 146 us
where the time goes in v1:
time: 661 us; the launch traced here: 660 us
  waiting for transfers between devices  424 us (64%)
  blocking collectives  123 us (19%)
  other arithmetic  40.1 us (6%)
  matrix products  27.7 us (4%)
  local copies, waits for them, and re-layouts  23.2 us (4%)
  between operations  14.9 us (2%)
  starting transfers between devices  7.5 us (1%)
    unnamed x7, waiting for transfers between devices  146 us
    psum x1, waiting for transfers between devices, on_device(): lax.psum(head_part.astype(jnp.bfloat16), 'head').astype(jnp.float32)  92.6 us
    psum x1, waiting for transfers between devices, on_device(): lax.psum(local_outputs.astype(jnp.bfloat16), 'seq').astype(jnp.float32)  83.4 us
    psum x1, waiting for transfers between devices, on_device(): lax.psum((query_part, kv_part, logit_part, squares, counts), 'seq')  53.4 us
    psum x1, blocking collectives, on_device(): lax.psum((query_part, kv_part, logit_part, squares, counts), 'seq')  50.9 us
    all_to_all x1, waiting for transfers between devices, on_device(): lax.all_to_all(jnp.stack([residual] * lax.axis_size('seq')), 'seq', 0, 0)  48.3 us
    pmax x1, blocking collectives, on_device(): maxima = lax.pmax(local_best, 'seq')  48.3 us
    psum x1, blocking collectives, on_device(): lax.psum(local_totals.astype(jnp.bfloat16), 'seq').astype(jnp.float32)  23.6 us
  transfers between devices with their start and end apart: 6, of which 6 were waited for; matrix products, arithmetic and copies ran while one was open for 3% of the time, Pallas kernels for 0%

profile of v1, /device:TPU:2, one launch (start us, length us, event | category | flops | bytes accessed | tf_op | source)
XLA Modules:
  0.0 659.8 jit_solution(433342207678966102)
XLA Ops:
  7.2 1.1 copy.200
  8.3 0.2 copy.139
  8.5 2.0 fusion.80
  10.4 2.7 fusion.68
  13.3 5.5 convert_reduce_fusion
  18.8 0.1 fusion.47
  19.3 50.9 %all-reduce.1 = (f32[4,128]{1,0:T(4,128)S(1)}, f32[128]{0:T(128)S(1)}, f32[4,128,8]{1,2,0:T(8,128)S(1)}) all-reduce(f32[4,128]{1,0:T(4,128)S(1)} %fusion.47, f32[128]{0:T(128)S(1)} %convert_reduce_fusion, f32[4,128,8]{1,2,0:T(8,128)S(1)} %fusion.78), channel_id=1, replica_groups=mesh['seq'=16,'head'=16] {'seq'}, use_global_device_ids=true, to_apply=%region_3.0 | all-reduce | flops 4736 | bytes 37888 | tf_op jit(solution)/shard_map/psum | solution.py:80
  70.5 7.3 %select_reduce_fusion.2 = f32[4,128,2]{2,1,0:T(8,128)S(1)} fusion(f32[4,128,8]{2,1,0:T(8,128)S(1)} %copy.151, s32[4,128,2]{2,1,0:T(8,128)S(1)} %copy.138), kind=kLoop, calls=%fused_computation.49 | loop fusion | flops 23552 | bytes 24576 | tf_op jit(solution)/shard_map/reduce_sum | solution.py:86
  77.8 0.8 fusion.105
  78.8 1.0 multiply_cosine_fusion.1
  79.7 53.4 %all-reduce.14.cloned.1.call-done = (f32[4,128,256]{2,1,0:T(8,128)}, f32[4,128,8,128]{3,1,2,0:T(8,128)}) async-done(((f32[4,128,256]{2,1,0:T(8,128)}, f32[4,128,8,128]{3,1,2,0:T(8,128)}), (f32[4,128,256]{2,1,0:T(8,128)}, f32[4,128,8,128]{3,1,2,0:T(8,128)})) %all-reduce.14.cloned.1.call-update) | async-done | bytes 2621456 | tf_op jit(solution)/shard_map/psum | solution.py:80
  133.2 1.3 multiply_bitcast_fusion
  134.5 1.2 fusion.43
  135.8 3.2 fusion.13
  138.9 0.8 subtract_convert_fusion
  139.8 0.7 maximum_bitcast_fusion
  140.5 0.2 copy.142
  140.7 0.7 gather_fusion
  141.4 3.7 fusion.103
  145.1 0.2 select_reduce_fusion.3
  145.5 0.5 fusion.104
  146.0 48.3 %pmax.7 = f32[128,1,8]{2,0,1:T(8,128)S(1)} all-reduce(f32[128,1,8]{2,0,1:T(8,128)S(1)} %maximum_bitcast_fusion.4), channel_id=1, replica_groups=mesh['seq'=16,'head'=16] {'seq'}, use_global_device_ids=true, to_apply=%region_10.0 | all-reduce | flops 1024 | bytes 8192 | tf_op jit(solution)/shard_map/pmax | solution.py:146
  194.3 0.6 gather_fusion.1
  194.9 0.3 fusion.40
  195.2 2.9 fusion.6
  198.0 0.3 fusion.64
  198.4 0.7 fusion.66
  199.1 1.3 fusion.22
  200.5 0.2 fusion.27
  200.7 23.6 %psum.61 = bf16[128,8]{0,1:T(8,128)(2,1)S(1)} all-reduce(bf16[128,8]{0,1:T(8,128)(2,1)S(1)} %fusion.27), channel_id=1, replica_groups=mesh['seq'=16,'head'=16] {'seq'}, use_global_device_ids=true, to_apply=%region_14.15 | all-reduce | flops 1024 | bytes 4096 | tf_op jit(solution)/shard_map/psum | solution.py:171
  224.3 83.4 %all-reduce.8.cloned.1.call-done = bf16[128,1,8,128]{3,0,2,1:T(8,128)(2,1)} async-done(((bf16[128,1,8,128]{3,0,2,1:T(8,128)(2,1)}), bf16[128,1,8,128]{3,0,2,1:T(8,128)(2,1)}) %all-reduce.8.cloned.1.call-update) | async-done | bytes 262160 | tf_op jit(solution)/shard_map/psum | solution.py:172
  307.6 1.2 convert_divide_fusion
  308.8 2.7 convolution_convert_fusion
  311.6 1.1 fusion.26
  312.7 92.6 %all-reduce.10.cloned.1.call-done = bf16[4,128,128]{2,1,0:T(8,128)(2,1)} async-done(((bf16[4,128,128]{2,1,0:T(8,128)(2,1)}), bf16[4,128,128]{2,1,0:T(8,128)(2,1)}) %all-reduce.10.cloned.1.call-update) | async-done | bytes 131088 | tf_op jit(solution)/shard_map/psum | solution.py:187
  405.3 0.9 fusion.48
  406.2 1.8 stack.2
  408.0 7.3 %all-to-all-start = ((bf16[16,4,128,128]{3,2,1,0:T(8,128)(2,1)}), bf16[16,4,128,128]{3,2,1,0:T(8,128)(2,1)}, u32[]{:S(2)}, u32[]{:S(2)}) async-start(bf16[16,4,128,128]{3,2,1,0:T(8,128)(2,1)} %stack.2), calls=%async_computation | async-start | bytes 4194304 | tf_op jit(solution)/shard_map/all_to_all | solution.py:190
  415.4 0.8 copy.155
  416.2 48.3 %all-to-all-done = bf16[16,4,128,128]{3,2,1,0:T(8,128)(2,1)} async-done(((bf16[16,4,128,128]{3,2,1,0:T(8,128)(2,1)}), bf16[16,4,128,128]{3,2,1,0:T(8,128)(2,1)}, u32[]{:S(2)}, u32[]{:S(2)}) %all-to-all-start) | async-done | bytes 2097184 | tf_op jit(solution)/shard_map/all_to_all | solution.py:190
  464.5 3.0 copy.153
  467.6 0.4 multiply_reduce_fusion
  468.0 2.5 convert_bitcast_fusion
  470.5 0.6 fusion.5
  471.3 0.7 fusion.86
  472.0 0.2 copy-done.1
  472.2 7.3 %select_reduce_fusion.1 = f32[4,128,2]{2,1,0:T(8,128)S(1)} fusion(f32[4,128,8]{2,1,0:T(8,128)S(1)} %fusion.86, s32[4,128,2]{2,1,0:T(8,128)S(1)} %copy-done.1), kind=kLoop, calls=%fused_computation.47 | loop fusion | flops 23552 | bytes 24576 | tf_op jit(solution)/shard_map/reduce_sum | solution.py:199
  479.5 0.2 fusion.73
  479.7 1.4 select_reduce_fusion
  481.2 5.4 copy.154
  486.8 4.1 fusion.3
  490.9 1.6 fusion.106
  492.5 4.2 multiply_convert_fusion
  496.6 3.1 copy.164
  499.7 1.7 copy.199
  501.5 0.6 copy-done.18
  502.1 0.6 dynamic-slice
  503.5 54.8 %reduce-scatter.5.cloned.1.call-done = bf16[128,512]{1,0:T(8,128)(2,1)} async-done(((bf16[2048,512]{1,0:T(8,128)(2,1)}), bf16[128,512]{1,0:T(8,128)(2,1)}) %reduce-scatter.5.cloned.1.call-update) | async-done | bytes 131088
  558.3 0.9 reshape.481
  559.3 0.8 copy.165
  560.1 0.3 convolution_convert_fusion.1
  560.4 0.6 copy.159
  561.0 90.9 %all-reduce.12.cloned.1.call-done = bf16[4,128,128]{2,1,0:T(8,128)(2,1)} async-done(((bf16[4,128,128]{2,1,0:T(8,128)(2,1)}), bf16[4,128,128]{2,1,0:T(8,128)(2,1)}) %all-reduce.12.cloned.1.call-update) | async-done | bytes 131088
  651.9 1.3 add_convert_fusion.1
  (74 shorter events, 2.0 us)
Async XLA Ops:
  7.2 485.3 %copy-start = (bf16[176,2048]{1,0:T(8,128)(2,1)S(1)}, bf16[176,2048]{1,0:T(8,128)(2,1)}, u32[]{:S(2)}) copy-start(bf16[176,2048]{1,0:T(8,128)(2,1)} %param.26) | copy-start | bytes 2162692
  7.2 126.0 %all-reduce.14.cloned.1.call-start = ((), (), s32[]{:S(2)}) async-start(), calls=%async_computation.6 | async-start | bytes 5242880 | tf_op jit(solution)/shard_map/psum | solution.py:80
  10.4 2.8 copy-start.7
  10.4 8.4 %copy-start.2 = (bf16[4,128,128]{2,1,0:T(8,128)(2,1)S(1)}, bf16[4,128,128]{2,1,0:T(8,128)(2,1)}, u32[]{:S(2)}) copy-start(bf16[4,128,128]{2,1,0:T(8,128)(2,1)} %param.16) | copy-start | bytes 393220
  10.4 8.7 %copy-start.11 = (f32[128]{0:T(128)S(1)}, f32[128]{0:T(128)}, u32[]{:S(2)}) copy-start(f32[128]{0:T(128)} %param.17) | copy-start | bytes 1540
  10.4 8.7 %copy-start.17 = (bf16[128,8]{0,1:T(8,128)(2,1)S(1)}, bf16[128,8]{0,1:T(8,128)(2,1)}, u32[]{:S(2)}) copy-start(bf16[128,8]{0,1:T(8,128)(2,1)} %param.18) | copy-start | bytes 6148
  13.1 6.1 copy-start.12
  13.1 57.2 %copy-start.9 = (s32[4,128,2]{1,2,0:T(2,128)S(1)}, s32[4,128,2]{1,2,0:T(2,128)}, u32[]{:S(2)}) copy-start(s32[4,128,2]{1,2,0:T(2,128)} %param.29) | copy-start | bytes 12292
  13.2 294.5 %all-reduce.8.cloned.1.call-start = ((), (), s32[]{:S(2)}) async-start(), calls=%async_computation.2 | async-start | bytes 524288 | tf_op jit(solution)/shard_map/psum | solution.py:172
  133.2 2.6 copy-start.13
  135.7 9.6 %copy-start.3 = (bf16[4,128,1,64]{3,1,0,2:T(8,128)(2,1)}, bf16[4,128,1,64]{3,1,0,2:T(8,128)(2,1)S(1)}, u32[]{:S(2)}) copy-start(bf16[4,128,1,64]{3,1,0,2:T(8,128)(2,1)S(1)} %get-tuple-element.27) | copy-start | bytes 196612
  135.7 9.6 %copy-start.5 = (bf16[4,128,1,64]{3,1,0,2:T(8,128)(2,1)}, bf16[4,128,1,64]{3,1,0,2:T(8,128)(2,1)S(1)}, u32[]{:S(2)}) copy-start(bf16[4,128,1,64]{3,1,0,2:T(8,128)(2,1)S(1)} %get-tuple-element.28) | copy-start | bytes 196612
  200.4 204.8 %all-reduce.10.cloned.1.call-start = ((), (), s32[]{:S(2)}) async-start(), calls=%async_computation.3 | async-start | bytes 262144 | tf_op jit(solution)/shard_map/psum | solution.py:187
  308.8 2.7 copy-start.15
  408.0 7.4 %copy-start.10 = (s32[4,128,2]{1,2,0:T(2,128)S(1)}, s32[4,128,2]{1,2,0:T(2,128)}, u32[]{:S(2)}) copy-start(s32[4,128,2]{1,2,0:T(2,128)} %param.30) | copy-start | bytes 12292
  408.0 56.5 %all-to-all-start = ((bf16[16,4,128,128]{3,2,1,0:T(8,128)(2,1)}), bf16[16,4,128,128]{3,2,1,0:T(8,128)(2,1)}, u32[]{:S(2)}, u32[]{:S(2)}) async-start(bf16[16,4,128,128]{3,2,1,0:T(8,128)(2,1)} %stack.2), calls=%async_computation | async-start | bytes 4194304 | tf_op jit(solution)/shard_map/all_to_all | solution.py:190
  415.3 143.0 %reduce-scatter.5.cloned.1.call-start = ((), (), s32[]{:S(2)}) async-start(), calls=%async_computation.4 | async-start | bytes 2228224
  468.0 2.5 copy-start.8
  470.5 0.8 copy-start.16
  471.3 0.9 copy-start.1
  486.8 4.1 copy-start.14
  501.4 0.7 copy-start.18
  501.4 58.6 %copy-start.4 = (bf16[4,128,1,64]{3,1,0,2:T(8,128)(2,1)S(1)}, bf16[4,128,1,64]{3,1,0,2:T(8,128)(2,1)}, u32[]{:S(2)}) copy-start(bf16[4,128,1,64]{3,1,0,2:T(8,128)(2,1)} %copy-done.3) | copy-start | bytes 196612
  501.4 58.7 %copy-start.6 = (bf16[4,128,1,64]{3,1,0,2:T(8,128)(2,1)S(1)}, bf16[4,128,1,64]{3,1,0,2:T(8,128)(2,1)}, u32[]{:S(2)}) copy-start(bf16[4,128,1,64]{3,1,0,2:T(8,128)(2,1)} %copy-done.5) | copy-start | bytes 196612
  501.5 150.5 %all-reduce.12.cloned.1.call-start = ((), (), s32[]{:S(2)}) async-start(), calls=%async_computation.5 | async-start | bytes 262144
Sparse Core Ops, SparseCore 0:
  13.3 119.8 all-reduce.13
  200.6 107.0 all-reduce.7
  312.8 92.4 all-reduce.9
  501.6 56.7 reduce-scatter.4
  561.4 90.4 all-reduce.11
